TPU v7x, 256 devices: a whole 4x4x8 slice. The times are simulated.
256 devices in a mesh: dp: 8 (over z), seq: 32 (over y, x, core).
Axes of the slice: x: 4, y: 4, z: 8, core: 2. Of those that a mesh axis runs over, the one named last changes fastest.
Arguments:
- inputs: bfloat16 [8, 4096, 2048], P('dp', 'seq'), may hold values from -6 to 6
- weight_codes: bfloat16 [2048, 1280], P('seq'), may hold values from -4 to 4
- scales: bfloat16 [2048, 10], P('seq'), may hold values from 0.010986328 to 0.043945312
- log_decay: float32 [8, 16, 4096], P('dp', None, 'seq'), may hold values from -0.85 to 0, as said below
- cotangent: bfloat16 [8, 4096, 1024], P('dp', 'seq'), may hold values from -6 to 6
Outputs:
- grad_inputs: float32 [8, 4096, 2048], P('dp', 'seq')
- grad_weight: float32 [2048, 1280], P('seq')
Inputs may be any that keep to these rules, and one draw needn't show every extreme that they name: log_decay is negative everywhere.
All inputs are finite; a program needn't handle non-finite values.
Results may differ from a plain program's by a relative error of at most 0.017.
Values may be sent and summed in bfloat16 or wider, within the bound.
No kernel may reach another device: no remote copies, remote signals or barrier semaphores. Data moves between devices by JAX's collectives and lax.ppermute only.
A program may use at most 128 MiB of HBM per device.

v0:
```python
import math
import jax
import jax.numpy as jnp
from jax import lax
from jax.sharding import PartitionSpec as P


def shifted(value, axis, step, reverse):
    count = lax.axis_size(axis)
    if reverse:
        pairs = [(place, place - step) for place in range(step, count)]
    else:
        pairs = [(place, place + step) for place in range(count - step)]
    return lax.ppermute(value, axis, pairs)


def scan_entering(decay, state, axis, reverse):
    head_count = state.shape[0]
    packed = jnp.concatenate(
        [state.reshape(head_count, -1), jnp.broadcast_to(decay[:, None], (head_count, 128))], axis=1
    )
    split = packed.shape[1] - 128
    packed = shifted(packed, axis, 1, reverse)
    step = 1
    while step < lax.axis_size(axis):
        earlier = shifted(packed, axis, step, reverse)
        later_decay = packed[:, split:]
        packed = jnp.concatenate(
            [
                later_decay[:, :1] * earlier[:, :split] + packed[:, :split],
                earlier[:, split:] * later_decay,
            ],
            axis=1,
        )
        step *= 2
    return packed[:, :split].reshape(state.shape)


def dequantize(code_rows, scale_rows):
    row_count, col_count = code_rows.shape
    group_count = scale_rows.shape[1]
    spread = code_rows.astype(jnp.float32).reshape(row_count, group_count, col_count // group_count)
    spread = spread * scale_rows.astype(jnp.float32)[:, :, None]
    return spread.reshape(row_count, col_count).astype(jnp.bfloat16)


def block_prep(ld_block):
    cum_log = jnp.cumsum(ld_block, axis=1)
    input_scale = jnp.sqrt(-jnp.expm1(2.0 * ld_block))
    tail_weight = jnp.exp(cum_log[:, -1:] - cum_log) * input_scale
    return (cum_log, input_scale, tail_weight)


def weighted_pair(x_vals, grad_out, tail_weight, cum_log, inv_root):
    head_weight = jnp.exp(cum_log) * inv_root
    weighted_x = (x_vals.astype(jnp.float32) * tail_weight.T[:, :, None]).astype(jnp.bfloat16)
    weighted_g = (grad_out.astype(jnp.float32) * head_weight.T[:, :, None]).astype(jnp.bfloat16)
    return (weighted_x, weighted_g)


def summaries(x_vals, b_mat, c_mat, grad_out, ld_block):
    cum_log, input_scale, tail_weight = block_prep(ld_block)
    inv_root = 1.0 / math.sqrt(b_mat.shape[1])
    weighted_x, weighted_g = weighted_pair(x_vals, grad_out, tail_weight, cum_log, inv_root)
    fwd_state = jnp.einsum("sn,shp->hnp", b_mat, weighted_x, preferred_element_type=jnp.float32)
    back_state = jnp.einsum("tn,thp->hnp", c_mat, weighted_g, preferred_element_type=jnp.float32)
    return (jnp.exp(cum_log[:, -1]), fwd_state, back_state)


def block_grads(x_vals, b_mat, c_mat, grad_out, ld_block, state_in, back_in):
    block_len = ld_block.shape[1]
    cum_log, input_scale, tail_weight = block_prep(ld_block)
    inv_root = 1.0 / math.sqrt(b_mat.shape[1])
    weighted_x, weighted_g = weighted_pair(x_vals, grad_out, tail_weight, cum_log, inv_root)
    row_ids = lax.broadcasted_iota(jnp.int32, (block_len, block_len), 0)
    col_ids = lax.broadcasted_iota(jnp.int32, (block_len, block_len), 1)
    lower_mask = (row_ids >= col_ids)[None]
    log_gap = cum_log[:, :, None] - cum_log[:, None, :]
    decay_mat = jnp.where(lower_mask, jnp.exp(jnp.where(lower_mask, log_gap, 0.0)), 0.0)
    state_low = state_in.astype(jnp.bfloat16)
    back_low = back_in.astype(jnp.bfloat16)
    x_dot_g = jnp.einsum("thp,shp->hts", grad_out, x_vals, preferred_element_type=jnp.float32)
    c_dot_b = jnp.dot(c_mat, b_mat.T, preferred_element_type=jnp.float32)
    mix_weights = (
        jnp.sum(decay_mat * input_scale[:, None, :] * x_dot_g, axis=0) * inv_root
    ).astype(jnp.bfloat16)
    d_c = jnp.einsum("hnp,thp->tn", state_low, weighted_g, preferred_element_type=jnp.float32)
    d_c = d_c + jnp.dot(mix_weights, b_mat, preferred_element_type=jnp.float32)
    d_b = jnp.einsum("hnp,thp->tn", back_low, weighted_x, preferred_element_type=jnp.float32)
    d_b = d_b + jnp.dot(mix_weights.T, c_mat, preferred_element_type=jnp.float32)
    d_x = (
        jnp.einsum("tn,hnp->thp", b_mat, back_low, preferred_element_type=jnp.float32)
        * tail_weight.T[:, :, None]
    )
    inner_weights = (decay_mat * c_dot_b[None] * inv_root).astype(jnp.bfloat16)
    inner = jnp.einsum("hus,uhp->shp", inner_weights, grad_out, preferred_element_type=jnp.float32)
    d_x = d_x + input_scale.T[:, :, None] * inner
    return (d_x, d_b, d_c)


def state_chain(decays, adds, start, backward):

    def step(carry, item):
        return (item[0][:, None, None] * carry + item[1], carry)

    return lax.scan(step, start, (decays, adds), reverse=backward)


def local(inputs, weight_codes, scales, log_decay, cotangent):
    tok_count = inputs.shape[1]
    features = inputs[0]
    grad_out = cotangent[0]
    head_count = log_decay.shape[1]
    hp_width = grad_out.shape[1]
    head_dim = hp_width // head_count
    proj_width = weight_codes.shape[1]
    state_width = (proj_width - hp_width) // 2
    weights = lax.all_gather(dequantize(weight_codes, scales), "seq", axis=0, tiled=True)
    projected = jnp.dot(features, weights, preferred_element_type=jnp.float32).astype(jnp.bfloat16)
    block_len = min(128, tok_count)
    block_count = tok_count // block_len
    x_blocks = projected[:, :hp_width].reshape(block_count, block_len, head_count, head_dim)
    b_blocks = projected[:, hp_width : hp_width + state_width].reshape(
        block_count, block_len, state_width
    )
    c_blocks = projected[:, hp_width + state_width :].reshape(block_count, block_len, state_width)
    g_blocks = grad_out.reshape(block_count, block_len, head_count, head_dim)
    ld_blocks = log_decay[0].reshape(head_count, block_count, block_len).transpose(1, 0, 2)
    decays, fwd_states, back_states = jax.vmap(summaries)(
        x_blocks, b_blocks, c_blocks, g_blocks, ld_blocks
    )
    zero_state = jnp.zeros((head_count, state_width, head_dim), jnp.float32)
    dev_decay = jnp.prod(decays, axis=0)
    dev_fwd, unused_a = state_chain(decays, fwd_states, zero_state, False)
    dev_back, unused_b = state_chain(decays, back_states, zero_state, True)
    carried = (None, scan_entering(dev_decay, dev_fwd, "seq", False))
    returned = (None, scan_entering(dev_decay, dev_back, "seq", True))
    unused_c, state_starts = state_chain(decays, fwd_states, carried[1], False)
    unused_d, back_starts = state_chain(decays, back_states, returned[1], True)
    d_x, d_b, d_c = lax.map(
        lambda block_item: block_grads(*block_item),
        (x_blocks, b_blocks, c_blocks, g_blocks, ld_blocks, state_starts, back_starts),
    )
    d_proj = jnp.concatenate(
        [
            d_x.reshape(tok_count, hp_width),
            d_b.reshape(tok_count, state_width),
            d_c.reshape(tok_count, state_width),
        ],
        axis=1,
    ).astype(jnp.bfloat16)
    grad_in = lax.dot_general(
        d_proj, weights, (((1,), (1,)), ((), ())), preferred_element_type=jnp.float32
    )
    seq_count = lax.axis_size("seq")
    group_count = lax.axis_size("dp")
    norm_factor = 1.0 / math.sqrt(group_count * seq_count * tok_count)
    partial_grad = lax.psum_scatter(
        lax.dot_general(
            features, d_proj, (((0,), (0,)), ((), ())), preferred_element_type=jnp.float32
        ),
        "seq",
        scatter_dimension=0,
        tiled=True,
    )
    summed_grad = lax.psum(partial_grad, "dp")
    return (grad_in[None], summed_grad * norm_factor)


def solution(mesh):
    placed = (
        P("dp", "seq", None),
        P("seq", None),
        P("seq", None),
        P("dp", None, "seq"),
        P("dp", "seq", None),
    )
    return jax.shard_map(
        local,
        mesh=mesh,
        in_specs=placed,
        out_specs=(P("dp", "seq", None), P("seq", None)),
        check_vma=False,
    )
```

profile of v0, /device:TPU:2, one launch (start us, length us, event | category | flops | bytes accessed | tf_op | source)
XLA Modules:
  0.0 389.5 jit_solution(13289274053930057519)
XLA Ops:
  7.2 0.8 copy.49
  8.2 1.7 fusion.30
  10.0 1.0 reduce_window_sum.23
  11.0 1.0 reduce_window_sum.24
  12.0 1.1 copy.50
  13.5 0.8 multiply_bitcast_fusion.3
  14.2 1.3 fusion.48
  15.7 50.6 %all-gather.2.cloned.1.call-done = bf16[2048,1280]{1,0:T(8,128)(2,1)} async-done(((bf16[64,1280]{1,0:T(8,128)(2,1)}), bf16[2048,1280]{1,0:T(8,128)(2,1)}) %all-gather.2.cloned.1.call-update) | async-done | bytes 5242896 | tf_op jit(solution)/shard_map/all_gather | solution.py:118
  66.2 4.1 %fusion = bf16[128,1280]{0,1:T(8,128)(2,1)S(1)} fusion(bf16[2048,1280]{1,0:T(8,128)(2,1)} %all-gather.2.cloned.1.call-done, bf16[1,128,2048]{2,1,0:T(8,128)(2,1)S(1)} %copy-done), kind=kOutput, calls=%fused_computation.3 | convolution fusion | flops 671252480 | bytes 6094848 | tf_op jit(solution)/shard_map/dot_general | solution.py:119
  70.5 0.8 fusion.10
  73.2 2.7 collective-permute-start
  75.9 1.9 collective-permute-start.6
  77.9 4.8 %collective-permute-done = f32[16,8320]{1,0:T(8,128)S(1)} collective-permute-done((f32[16,8320]{1,0:T(8,128)S(1)}, f32[16,8320]{1,0:T(8,128)S(1)}, u32[]{:S(2)}, u32[]{:S(2)}) %collective-permute-start) | collective-permute-done | bytes 532512 | tf_op jit(solution)/shard_map/ppermute | solution.py:14
  82.7 3.8 collective-permute-start.1
  86.5 0.9 fusion.2
  87.4 0.8 fusion.34
  88.3 1.9 collective-permute-start.7
  90.4 2.8 collective-permute-done.1
  93.4 1.9 collective-permute-start.2
  95.4 3.5 collective-permute-done.7
  99.0 3.3 collective-permute-start.8
  102.6 6.7 %collective-permute-done.2 = f32[16,8320]{1,0:T(8,128)S(1)} collective-permute-done((f32[16,8320]{1,0:T(8,128)S(1)}, f32[16,8320]{1,0:T(8,128)S(1)}, u32[]{:S(2)}, u32[]{:S(2)}) %collective-permute-start.2) | collective-permute-done | bytes 532512 | tf_op jit(solution)/shard_map/ppermute | solution.py:14
  109.5 1.3 collective-permute-start.3
  110.8 3.1 collective-permute-done.8
  114.1 19.8 %collective-permute-start.9 = (f32[16,8320]{1,0:T(8,128)S(1)}, f32[16,8320]{1,0:T(8,128)S(1)}, u32[]{:S(2)}, u32[]{:S(2)}) collective-permute-start(f32[16,8320]{1,0:T(8,128)S(1)} %pad_maximum_fusion.7), channel_id=1, source_target_pairs={{0,4},{1,5},{2,6},{3,7},{4,8},{5,9},{6,10},{7,11},{8,12},{9,13},{1... | collective-permute-start | bytes 1597448 | tf_op jit(solution)/shard_map/ppermute | solution.py:14
  134.4 1.3 collective-permute-start.4
  135.7 7.2 %collective-permute-done.9 = f32[16,8320]{1,0:T(8,128)S(1)} collective-permute-done((f32[16,8320]{1,0:T(8,128)S(1)}, f32[16,8320]{1,0:T(8,128)S(1)}, u32[]{:S(2)}, u32[]{:S(2)}) %collective-permute-start.9) | collective-permute-done | bytes 532512 | tf_op jit(solution)/shard_map/ppermute | solution.py:14
  143.1 5.6 %collective-permute-start.10 = (f32[16,8320]{1,0:T(8,128)S(1)}, f32[16,8320]{1,0:T(8,128)S(1)}, u32[]{:S(2)}, u32[]{:S(2)}) collective-permute-start(f32[16,8320]{1,0:T(8,128)S(1)} %pad_maximum_fusion.8), channel_id=1, source_target_pairs={{0,8},{1,9},{2,10},{3,11},{4,12},{5,13},{6,14},{7,15},{8,16},{9,17... | collective-permute-start | bytes 1597448 | tf_op jit(solution)/shard_map/ppermute | solution.py:14
  149.6 1.3 collective-permute-start.5
  150.9 4.6 %collective-permute-done.10 = f32[16,8320]{1,0:T(8,128)S(1)} collective-permute-done((f32[16,8320]{1,0:T(8,128)S(1)}, f32[16,8320]{1,0:T(8,128)S(1)}, u32[]{:S(2)}, u32[]{:S(2)}) %collective-permute-start.10) | collective-permute-done | bytes 532512 | tf_op jit(solution)/shard_map/ppermute | solution.py:14
  155.7 10.0 %collective-permute-start.11 = (f32[16,8320]{1,0:T(8,128)S(1)}, f32[16,8320]{1,0:T(8,128)}, u32[]{:S(2)}, u32[]{:S(2)}) collective-permute-start(f32[16,8320]{1,0:T(8,128)S(1)} %pad_maximum_fusion.9), channel_id=1, source_target_pairs={{0,16},{1,17},{2,18},{3,19},{4,20},{5,21},{6,22},{7,23},{8,24},{9,... | collective-permute-start | bytes 1597448 | tf_op jit(solution)/shard_map/ppermute | solution.py:14
  165.8 0.6 slice_reduce_fusion.1
  166.4 2.6 collective-permute-done.5
  169.1 0.5 convert_element_type.100
  169.9 0.9 convolution_bitcast_fusion.7
  171.0 0.6 collective-permute-done.11
  171.7 1.2 fusion.13
  172.8 0.5 convert_element_type.111
  173.4 1.0 fusion.6
  174.8 1.4 fusion.5
  176.3 5.3 %convolution_bitcast_fusion = f32[2048,1280]{0,1:T(8,128)} fusion(bf16[1,128,2048]{2,1,0:T(8,128)(2,1)S(1)} %copy-done, bf16[128,128]{0,1:T(8,128)(2,1)S(1)} %fusion.7, bf16[128,128]{0,1:T(8,128)(2,1)S(1)} %fusion.6, bf16[128,1024]{0,1:T(8,128)(2,1)S(1)} %bitcast.105), kind=kOutput, calls=%fused_computation | convolution fusion | flops 672071680 | bytes 11337728 | tf_op jit(solution)/shard_map/dot_general | solution.py:159
  181.6 11.3 %copy.72 = f32[2048,1280]{1,0:T(8,128)} copy(f32[2048,1280]{0,1:T(8,128)} %convolution_bitcast_fusion) | data formatting | bytes 20971520
  193.0 111.7 %reduce-scatter.4.cloned.1.call-done = f32[64,1280]{1,0:T(8,128)} async-done(((f32[2048,1280]{1,0:T(8,128)}), f32[64,1280]{1,0:T(8,128)}) %reduce-scatter.4.cloned.1.call-update) | async-done | bytes 327696
  304.7 2.0 copy.73
  306.8 5.3 %convolution_bitcast_fusion.1 = f32[1,128,2048]{2,1,0:T(8,128)} fusion(bf16[2048,1280]{1,0:T(8,128)(2,1)} %all-gather.2.cloned.1.call-done, bf16[128,128]{0,1:T(8,128)(2,1)S(1)} %fusion.7, bf16[128,128]{0,1:T(8,128)(2,1)S(1)} %fusion.6, bf16[128,1024]{0,1:T(8,128)(2,1)S(1)} %bitcast.106), kind=kOutput, calls=%fused_computation.1 | convolution fusion | flops 672071680 | bytes 6619136 | tf_op jit(solution)/shard_map/dot_general | solution.py:152
  312.1 68.8 %all-reduce.2.cloned.1.call-done = f32[64,1280]{0,1:T(8,128)} async-done(((f32[64,1280]{0,1:T(8,128)}), f32[64,1280]{0,1:T(8,128)}) %all-reduce.2.cloned.1.call-update) | async-done | bytes 327696 | tf_op jit(solution)/shard_map/psum | solution.py:166
  380.9 1.1 broadcast_multiply_fusion
  382.1 0.9 copy.62
  (71 shorter events, 6.8 us)
Async XLA Ops:
  7.2 59.1 %copy-start = (bf16[1,128,2048]{2,1,0:T(8,128)(2,1)S(1)}, bf16[1,128,2048]{2,1,0:T(8,128)(2,1)}, u32[]{:S(2)}) copy-start(bf16[1,128,2048]{2,1,0:T(8,128)(2,1)} %param.5) | copy-start | bytes 1572868
  7.2 59.0 %all-gather.2.cloned.1.call-start = ((), (), s32[]{:S(2)}) async-start(), calls=%async_computation.1 | async-start | bytes 5406720 | tf_op jit(solution)/shard_map/all_gather | solution.py:118
  10.0 294.7 %reduce-scatter.4.cloned.1.call-start = ((), (), s32[]{:S(2)}) async-start(), calls=%async_computation.3 | async-start | bytes 10813440
  15.6 55.8 %copy-start.2 = (f32[128,16]{0,1:T(8,128)}, f32[128,16]{0,1:T(8,128)S(1)}, u32[]{:S(2)}) copy-start(f32[128,16]{0,1:T(8,128)S(1)} %get-tuple-element.80) | copy-start | bytes 24580
  73.2 9.4 %collective-permute-start = (f32[16,8320]{1,0:T(8,128)S(1)}, f32[16,8320]{1,0:T(8,128)S(1)}, u32[]{:S(2)}, u32[]{:S(2)}) collective-permute-start(f32[16,8320]{1,0:T(8,128)S(1)} %get-tuple-element.94), channel_id=1, source_target_pairs={{1,0},{2,1},{3,2},{4,3},{5,4},{6,5},{7,6},{8,7},{9,8},{10,9},{11,1... | collective-permute-start | bytes 1597448 | tf_op jit(solution)/shard_map/ppermute | solution.py:14
  75.9 12.4 %collective-permute-start.6 = (f32[16,8320]{1,0:T(8,128)S(1)}, f32[16,8320]{1,0:T(8,128)S(1)}, u32[]{:S(2)}, u32[]{:S(2)}) collective-permute-start(f32[16,8320]{1,0:T(8,128)S(1)} %get-tuple-element.95), channel_id=1, source_target_pairs={{0,1},{1,2},{2,3},{3,4},{4,5},{5,6},{6,7},{7,8},{8,9},{9,10},{10,1... | collective-permute-start | bytes 1597448 | tf_op jit(solution)/shard_map/ppermute | solution.py:14
  77.9 31.6 %copy-start.3 = (pred[128,128]{0,1:T(8,128)(4,1)}, pred[128,128]{0,1:T(8,128)(4,1)S(1)}, u32[]{:S(2)}) copy-start(pred[128,128]{0,1:T(8,128)(4,1)S(1)} %iota_compare_fusion) | copy-start | bytes 49156
  82.7 10.6 %collective-permute-start.1 = (f32[16,8320]{1,0:T(8,128)S(1)}, f32[16,8320]{1,0:T(8,128)S(1)}, u32[]{:S(2)}, u32[]{:S(2)}) collective-permute-start(f32[16,8320]{1,0:T(8,128)S(1)} %collective-permute-done), channel_id=1, source_target_pairs={{1,0},{2,1},{3,2},{4,3},{5,4},{6,5},{7,6},{8,7},{9,8},{10,9},{11,1... | collective-permute-start | bytes 1597448 | tf_op jit(solution)/shard_map/ppermute | solution.py:14
  88.3 10.6 %collective-permute-start.7 = (f32[16,8320]{1,0:T(8,128)S(1)}, f32[16,8320]{1,0:T(8,128)S(1)}, u32[]{:S(2)}, u32[]{:S(2)}) collective-permute-start(f32[16,8320]{1,0:T(8,128)S(1)} %collective-permute-done.6), channel_id=1, source_target_pairs={{0,1},{1,2},{2,3},{3,4},{4,5},{5,6},{6,7},{7,8},{8,9},{9,10},{10,1... | collective-permute-start | bytes 1597448 | tf_op jit(solution)/shard_map/ppermute | solution.py:14
  93.4 15.9 %collective-permute-start.2 = (f32[16,8320]{1,0:T(8,128)S(1)}, f32[16,8320]{1,0:T(8,128)S(1)}, u32[]{:S(2)}, u32[]{:S(2)}) collective-permute-start(f32[16,8320]{1,0:T(8,128)S(1)} %pad_maximum_fusion.2), channel_id=1, source_target_pairs={{2,0},{3,1},{4,2},{5,3},{6,4},{7,5},{8,6},{9,7},{10,8},{11,9},{12,... | collective-permute-start | bytes 1597448 | tf_op jit(solution)/shard_map/ppermute | solution.py:14
  99.0 14.9 %collective-permute-start.8 = (f32[16,8320]{1,0:T(8,128)S(1)}, f32[16,8320]{1,0:T(8,128)S(1)}, u32[]{:S(2)}, u32[]{:S(2)}) collective-permute-start(f32[16,8320]{1,0:T(8,128)S(1)} %pad_maximum_fusion.6), channel_id=1, source_target_pairs={{0,2},{1,3},{2,4},{3,5},{4,6},{5,7},{6,8},{7,9},{8,10},{9,11},{10,... | collective-permute-start | bytes 1597448 | tf_op jit(solution)/shard_map/ppermute | solution.py:14
  109.5 24.7 %collective-permute-start.3 = (f32[16,8320]{1,0:T(8,128)S(1)}, f32[16,8320]{1,0:T(8,128)S(1)}, u32[]{:S(2)}, u32[]{:S(2)}) collective-permute-start(f32[16,8320]{1,0:T(8,128)S(1)} %pad_maximum_fusion.3), channel_id=1, source_target_pairs={{4,0},{5,1},{6,2},{7,3},{8,4},{9,5},{10,6},{11,7},{12,8},{13,9},{1... | collective-permute-start | bytes 1597448 | tf_op jit(solution)/shard_map/ppermute | solution.py:14
  114.1 28.8 %collective-permute-start.9 = (f32[16,8320]{1,0:T(8,128)S(1)}, f32[16,8320]{1,0:T(8,128)S(1)}, u32[]{:S(2)}, u32[]{:S(2)}) collective-permute-start(f32[16,8320]{1,0:T(8,128)S(1)} %pad_maximum_fusion.7), channel_id=1, source_target_pairs={{0,4},{1,5},{2,6},{3,7},{4,8},{5,9},{6,10},{7,11},{8,12},{9,13},{1... | collective-permute-start | bytes 1597448 | tf_op jit(solution)/shard_map/ppermute | solution.py:14
  134.4 15.0 %collective-permute-start.4 = (f32[16,8320]{1,0:T(8,128)S(1)}, f32[16,8320]{1,0:T(8,128)S(1)}, u32[]{:S(2)}, u32[]{:S(2)}) collective-permute-start(f32[16,8320]{1,0:T(8,128)S(1)} %pad_maximum_fusion.4), channel_id=1, source_target_pairs={{8,0},{9,1},{10,2},{11,3},{12,4},{13,5},{14,6},{15,7},{16,8},{17,9... | collective-permute-start | bytes 1597448 | tf_op jit(solution)/shard_map/ppermute | solution.py:14
  142.9 27.0 %copy-start.1 = (bf16[128,1024]{0,1:T(8,128)(2,1)S(1)}, bf16[128,1024]{0,1:T(8,128)(2,1)}, u32[]{:S(2)}) copy-start(bf16[128,1024]{0,1:T(8,128)(2,1)} %get-tuple-element.75) | copy-start | bytes 786436
  143.1 12.5 %collective-permute-start.10 = (f32[16,8320]{1,0:T(8,128)S(1)}, f32[16,8320]{1,0:T(8,128)S(1)}, u32[]{:S(2)}, u32[]{:S(2)}) collective-permute-start(f32[16,8320]{1,0:T(8,128)S(1)} %pad_maximum_fusion.8), channel_id=1, source_target_pairs={{0,8},{1,9},{2,10},{3,11},{4,12},{5,13},{6,14},{7,15},{8,16},{9,17... | collective-permute-start | bytes 1597448 | tf_op jit(solution)/shard_map/ppermute | solution.py:14
  149.6 19.3 %collective-permute-start.5 = (f32[16,8320]{1,0:T(8,128)S(1)}, f32[16,8320]{1,0:T(8,128)S(1)}, u32[]{:S(2)}, u32[]{:S(2)}) collective-permute-start(f32[16,8320]{1,0:T(8,128)S(1)} %pad_maximum_fusion.5), channel_id=1, source_target_pairs={{16,0},{17,1},{18,2},{19,3},{20,4},{21,5},{22,6},{23,7},{24,8},{25... | collective-permute-start | bytes 1597448 | tf_op jit(solution)/shard_map/ppermute | solution.py:14
  155.7 15.9 %collective-permute-start.11 = (f32[16,8320]{1,0:T(8,128)S(1)}, f32[16,8320]{1,0:T(8,128)}, u32[]{:S(2)}, u32[]{:S(2)}) collective-permute-start(f32[16,8320]{1,0:T(8,128)S(1)} %pad_maximum_fusion.9), channel_id=1, source_target_pairs={{0,16},{1,17},{2,18},{3,19},{4,20},{5,21},{6,22},{7,23},{8,24},{9,... | collective-permute-start | bytes 1597448 | tf_op jit(solution)/shard_map/ppermute | solution.py:14
  192.9 188.0 %all-reduce.2.cloned.1.call-start = ((), (), s32[]{:S(2)}) async-start(), calls=%async_computation.2 | async-start | bytes 1310720 | tf_op jit(solution)/shard_map/psum | solution.py:166
Sparse Core Ops, SparseCore 0:
  11.1 55.0 all-gather.1
  193.1 111.5 reduce-scatter.3
  307.2 73.7 all-reduce.1
where the time goes:
time: 391 us; the launch traced here: 390 us
  waiting for transfers between devices  268 us (69%)
  starting transfers between devices  55 us (14%)
  local copies, waits for them, and re-layouts  21.2 us (5%)
  matrix products  20.9 us (5%)
  between operations  14.1 us (4%)
  other arithmetic  10.7 us (3%)
    unnamed x4, waiting for transfers between devices  112 us
    psum x1, waiting for transfers between devices, local(): summed_grad = lax.psum(partial_grad, 'dp')  68.8 us
    ppermute x12, starting transfers between devices, shifted(): return lax.ppermute(value, axis, pairs)  54.8 us
    all_gather x1, waiting for transfers between devices, local(): lax.all_gather(dequantize(weight_codes, scales), 'seq', axis=0, tiled=True)  50.6 us
    ppermute x12, waiting for transfers between devices, shifted(): return lax.ppermute(value, axis, pairs)  36.5 us
    unnamed x12, local copies, waits for them, and re-layouts  15.4 us
  transfers between devices with their start and end apart: 15, of which 13 were waited for; matrix products, arithmetic and copies ran while one was open for 5% of the time, Pallas kernels for 0%

commit v1 on v0

--- a/solution.py
+++ b/solution.py
@@ -1,8 +1,21 @@
+import functools
 import math
 import jax
 import jax.numpy as jnp
 from jax import lax
 from jax.sharding import PartitionSpec as P
+
+
+def field_update(mat, group_axis):
+    leaves = []
+    for _ in range(lax.axis_size(group_axis)):
+        leaves.append(mat)
+    return jnp.concatenate(
+        lax.all_to_all(jnp.stack(leaves), axis_name=group_axis, split_axis=0, concat_axis=0), axis=0
+    )
+
+
+point_rounds = functools.partial(field_update, group_axis="seq")
 
 
 def shifted(value, axis, step, reverse):
@@ -115,7 +128,7 @@
     head_dim = hp_width // head_count
     proj_width = weight_codes.shape[1]
     state_width = (proj_width - hp_width) // 2
-    weights = lax.all_gather(dequantize(weight_codes, scales), "seq", axis=0, tiled=True)
+    weights = point_rounds(dequantize(weight_codes, scales))
     projected = jnp.dot(features, weights, preferred_element_type=jnp.float32).astype(jnp.bfloat16)
     block_len = min(128, tok_count)
     block_count = tok_count // block_len

time: 391 us -> 409 us (1.046)
  waiting for transfers between devices: 268 us -> 281 us
  starting transfers between devices: 55 us -> 61 us
    all_to_all x0 -> x1, waiting for transfers between devices: none -> 61.2 us  [field_update(): lax.all_to_all(jnp.stack(leaves), axis_name=group_axis, split_axis=0, con...]
    all_gather x1 -> x0, waiting for transfers between devices: 50.6 us -> none  [local(): lax.all_gather(dequantize(weight_codes, scales), 'seq', axis=0, tiled=True)]
    all_to_all x0 -> x1, starting transfers between devices: none -> 7.8 us  [field_update(): lax.all_to_all(jnp.stack(leaves), axis_name=group_axis, split_axis=0, con...]
    unnamed x4 -> x3, waiting for transfers between devices: 112 us -> 113 us
    unnamed x12 -> x16, local copies, waits for them, and re-layouts: 15.4 us -> 14.5 us
  transfers between devices with their start and end apart: 15 -> 15, of which waited for: 13 -> 13; matrix products, arithmetic and copies ran while one was open for 5% -> 3% of each run, Pallas kernels for 0% -> 0%
where the time goes in v1:
time: 409 us; the launch traced here: 408 us
  waiting for transfers between devices  281 us (69%)
  starting transfers between devices  61 us (15%)
  local copies, waits for them, and re-layouts  23.3 us (6%)
  matrix products  20.9 us (5%)
  between operations  14.5 us (4%)
  other arithmetic  7.21 us (2%)
    unnamed x3, waiting for transfers between devices  113 us
    psum x1, waiting for transfers between devices, local(): summed_grad = lax.psum(partial_grad, 'dp')  68.8 us
    all_to_all x1, waiting for transfers between devices, field_update(): lax.all_to_all(jnp.stack(leaves), axis_name=group_axis, split_axis=0, con...  61.2 us
    ppermute x12, starting transfers between devices, shifted(): return lax.ppermute(value, axis, pairs)  53.1 us
    ppermute x12, waiting for transfers between devices, shifted(): return lax.ppermute(value, axis, pairs)  37.9 us
    unnamed x16, local copies, waits for them, and re-layouts  14.5 us
  transfers between devices with their start and end apart: 15, of which 13 were waited for; matrix products, arithmetic and copies ran while one was open for 3% of the time, Pallas kernels for 0%

profile of v1, /device:TPU:2, one launch (start us, length us, event | category | flops | bytes accessed | tf_op | source)
XLA Modules:
  0.0 407.9 jit_solution(5325029210819385870)
XLA Ops:
  7.2 0.8 copy.49
  8.2 1.0 fusion.30
  9.2 2.9 stack.2
  12.1 7.8 %all-to-all-start = ((bf16[32,64,1280]{2,1,0:T(8,128)(2,1)}), bf16[32,64,1280]{2,1,0:T(8,128)(2,1)}, u32[]{:S(2)}, u32[]{:S(2)}) async-start(bf16[32,64,1280]{2,1,0:T(8,128)(2,1)} %stack.2), calls=%async_computation | async-start | bytes 10485760 | tf_op jit(solution)/shard_map/all_to_all | solution.py:14
  21.2 0.6 fusion.48
  21.9 61.2 %all-to-all-done = bf16[32,64,1280]{2,1,0:T(8,128)(2,1)} async-done(((bf16[32,64,1280]{2,1,0:T(8,128)(2,1)}), bf16[32,64,1280]{2,1,0:T(8,128)(2,1)}, u32[]{:S(2)}, u32[]{:S(2)}) %all-to-all-start) | async-done | bytes 5242912 | tf_op jit(solution)/shard_map/all_to_all | solution.py:14
  83.1 4.1 fusion
  87.4 0.8 fusion.10
  88.8 0.4 squeeze.57
  90.1 1.9 collective-permute-start
  92.0 2.4 collective-permute-start.6
  94.5 4.3 %collective-permute-done = f32[16,8320]{1,0:T(8,128)S(1)} collective-permute-done((f32[16,8320]{1,0:T(8,128)S(1)}, f32[16,8320]{1,0:T(8,128)S(1)}, u32[]{:S(2)}, u32[]{:S(2)}) %collective-permute-start) | collective-permute-done | bytes 532512 | tf_op jit(solution)/shard_map/ppermute | solution.py:27
  98.8 3.8 collective-permute-start.1
  102.6 0.9 fusion.2
  103.6 0.8 fusion.34
  104.4 2.1 collective-permute-start.7
  106.7 2.7 collective-permute-done.1
  109.6 1.9 collective-permute-start.2
  111.5 3.5 collective-permute-done.7
  115.2 3.7 collective-permute-start.8
  119.1 5.9 %collective-permute-done.2 = f32[16,8320]{1,0:T(8,128)S(1)} collective-permute-done((f32[16,8320]{1,0:T(8,128)S(1)}, f32[16,8320]{1,0:T(8,128)S(1)}, u32[]{:S(2)}, u32[]{:S(2)}) %collective-permute-start.2) | collective-permute-done | bytes 532512 | tf_op jit(solution)/shard_map/ppermute | solution.py:27
  125.2 1.3 collective-permute-start.3
  126.5 4.0 collective-permute-done.8
  130.6 20.8 %collective-permute-start.9 = (f32[16,8320]{1,0:T(8,128)S(1)}, f32[16,8320]{1,0:T(8,128)S(1)}, u32[]{:S(2)}, u32[]{:S(2)}) collective-permute-start(f32[16,8320]{1,0:T(8,128)S(1)} %pad_maximum_fusion.7), channel_id=1, source_target_pairs={{0,4},{1,5},{2,6},{3,7},{4,8},{5,9},{6,10},{7,11},{8,12},{9,13},{1... | collective-permute-start | bytes 1597448 | tf_op jit(solution)/shard_map/ppermute | solution.py:27
  151.9 1.3 collective-permute-start.4
  153.2 7.4 %collective-permute-done.9 = f32[16,8320]{1,0:T(8,128)S(1)} collective-permute-done((f32[16,8320]{1,0:T(8,128)S(1)}, f32[16,8320]{1,0:T(8,128)S(1)}, u32[]{:S(2)}, u32[]{:S(2)}) %collective-permute-start.9) | collective-permute-done | bytes 532512 | tf_op jit(solution)/shard_map/ppermute | solution.py:27
  160.7 4.4 %collective-permute-start.10 = (f32[16,8320]{1,0:T(8,128)S(1)}, f32[16,8320]{1,0:T(8,128)S(1)}, u32[]{:S(2)}, u32[]{:S(2)}) collective-permute-start(f32[16,8320]{1,0:T(8,128)S(1)} %pad_maximum_fusion.8), channel_id=1, source_target_pairs={{0,8},{1,9},{2,10},{3,11},{4,12},{5,13},{6,14},{7,15},{8,16},{9,17... | collective-permute-start | bytes 1597448 | tf_op jit(solution)/shard_map/ppermute | solution.py:27
  165.3 0.5 collective-permute-done.4
  166.0 1.3 collective-permute-start.5
  167.3 6.6 %collective-permute-done.10 = f32[16,8320]{1,0:T(8,128)S(1)} collective-permute-done((f32[16,8320]{1,0:T(8,128)S(1)}, f32[16,8320]{1,0:T(8,128)S(1)}, u32[]{:S(2)}, u32[]{:S(2)}) %collective-permute-start.10) | collective-permute-done | bytes 532512 | tf_op jit(solution)/shard_map/ppermute | solution.py:27
  174.1 8.2 %collective-permute-start.11 = (f32[16,8320]{1,0:T(8,128)S(1)}, f32[16,8320]{1,0:T(8,128)}, u32[]{:S(2)}, u32[]{:S(2)}) collective-permute-start(f32[16,8320]{1,0:T(8,128)S(1)} %pad_maximum_fusion.9), channel_id=1, source_target_pairs={{0,16},{1,17},{2,18},{3,19},{4,20},{5,21},{6,22},{7,23},{8,24},{9,... | collective-permute-start | bytes 1597448 | tf_op jit(solution)/shard_map/ppermute | solution.py:27
  182.4 0.7 slice_reduce_fusion.1
  183.1 2.5 collective-permute-done.5
  185.7 0.5 convert_element_type.100
  186.5 0.9 convolution_bitcast_fusion.7
  187.6 0.6 collective-permute-done.11
  188.3 1.2 fusion.13
  189.4 0.5 convert_element_type.111
  190.0 1.0 fusion.6
  191.4 1.4 fusion.5
  192.9 5.3 %convolution_bitcast_fusion = f32[2048,1280]{0,1:T(8,128)} fusion(bf16[1,128,2048]{2,1,0:T(8,128)(2,1)S(1)} %copy-done, bf16[128,128]{0,1:T(8,128)(2,1)S(1)} %fusion.7, bf16[128,128]{0,1:T(8,128)(2,1)S(1)} %fusion.6, bf16[128,1024]{0,1:T(8,128)(2,1)S(1)} %bitcast.106), kind=kOutput, calls=%fused_computation | convolution fusion | flops 672071680 | bytes 11337728 | tf_op jit(solution)/shard_map/dot_general | solution.py:172
  198.2 11.3 %copy.72 = f32[2048,1280]{1,0:T(8,128)} copy(f32[2048,1280]{0,1:T(8,128)} %convolution_bitcast_fusion) | data formatting | bytes 20971520
  209.6 113.2 %reduce-scatter.4.cloned.1.call-done = f32[64,1280]{1,0:T(8,128)} async-done(((f32[2048,1280]{1,0:T(8,128)}), f32[64,1280]{1,0:T(8,128)}) %reduce-scatter.4.cloned.1.call-update) | async-done | bytes 327696
  322.8 2.0 copy.73
  324.9 5.3 %convolution_bitcast_fusion.1 = f32[1,128,2048]{2,1,0:T(8,128)} fusion(bf16[2048,1280]{1,0:T(8,128)(2,1)} %bitcast, bf16[128,128]{0,1:T(8,128)(2,1)S(1)} %fusion.7, bf16[128,128]{0,1:T(8,128)(2,1)S(1)} %fusion.6, bf16[128,1024]{0,1:T(8,128)(2,1)S(1)} %bitcast.107), kind=kOutput, calls=%fused_computation.1 | convolution fusion | flops 672071680 | bytes 6619136 | tf_op jit(solution)/shard_map/dot_general | solution.py:165
  330.2 68.8 %all-reduce.2.cloned.1.call-done = f32[64,1280]{0,1:T(8,128)} async-done(((f32[64,1280]{0,1:T(8,128)}), f32[64,1280]{0,1:T(8,128)}) %all-reduce.2.cloned.1.call-update) | async-done | bytes 327696 | tf_op jit(solution)/shard_map/psum | solution.py:179
  399.0 1.1 broadcast_multiply_fusion
  400.1 0.9 copy.62
  (75 shorter events, 6.8 us)
Async XLA Ops:
  7.2 76.0 %copy-start = (bf16[1,128,2048]{2,1,0:T(8,128)(2,1)S(1)}, bf16[1,128,2048]{2,1,0:T(8,128)(2,1)}, u32[]{:S(2)}) copy-start(bf16[1,128,2048]{2,1,0:T(8,128)(2,1)} %param.5) | copy-start | bytes 1572868
  12.1 7.9 %copy-start.3 = (f32[1,16,128]{2,1,0:T(8,128)S(1)}, f32[1,16,128]{2,1,0:T(8,128)}, u32[]{:S(2)}) copy-start(f32[1,16,128]{2,1,0:T(8,128)} %param.8) | copy-start | bytes 24580
  12.1 8.4 %copy-start.2 = (bf16[1,128,1024]{2,1,0:T(8,128)(2,1)S(1)}, bf16[1,128,1024]{2,1,0:T(8,128)(2,1)}, u32[]{:S(2)}) copy-start(bf16[1,128,1024]{2,1,0:T(8,128)(2,1)} %param.9) | copy-start | bytes 786436
  12.1 71.0 %all-to-all-start = ((bf16[32,64,1280]{2,1,0:T(8,128)(2,1)}), bf16[32,64,1280]{2,1,0:T(8,128)(2,1)}, u32[]{:S(2)}, u32[]{:S(2)}) async-start(bf16[32,64,1280]{2,1,0:T(8,128)(2,1)} %stack.2), calls=%async_computation | async-start | bytes 10485760 | tf_op jit(solution)/shard_map/all_to_all | solution.py:14
  20.0 302.8 %reduce-scatter.4.cloned.1.call-start = ((), (), s32[]{:S(2)}) async-start(), calls=%async_computation.3 | async-start | bytes 10813440
  21.8 66.4 %copy-start.4 = (f32[128,16]{0,1:T(8,128)}, f32[128,16]{0,1:T(8,128)S(1)}, u32[]{:S(2)}) copy-start(f32[128,16]{0,1:T(8,128)S(1)} %get-tuple-element.80) | copy-start | bytes 24580
  90.1 8.7 %collective-permute-start = (f32[16,8320]{1,0:T(8,128)S(1)}, f32[16,8320]{1,0:T(8,128)S(1)}, u32[]{:S(2)}, u32[]{:S(2)}) collective-permute-start(f32[16,8320]{1,0:T(8,128)S(1)} %get-tuple-element.94), channel_id=1, source_target_pairs={{1,0},{2,1},{3,2},{4,3},{5,4},{6,5},{7,6},{8,7},{9,8},{10,9},{11,1... | collective-permute-start | bytes 1597448 | tf_op jit(solution)/shard_map/ppermute | solution.py:27
  92.0 12.4 %collective-permute-start.6 = (f32[16,8320]{1,0:T(8,128)S(1)}, f32[16,8320]{1,0:T(8,128)S(1)}, u32[]{:S(2)}, u32[]{:S(2)}) collective-permute-start(f32[16,8320]{1,0:T(8,128)S(1)} %get-tuple-element.95), channel_id=1, source_target_pairs={{0,1},{1,2},{2,3},{3,4},{4,5},{5,6},{6,7},{7,8},{8,9},{9,10},{10,1... | collective-permute-start | bytes 1597448 | tf_op jit(solution)/shard_map/ppermute | solution.py:27
  94.5 30.7 %copy-start.5 = (pred[128,128]{0,1:T(8,128)(4,1)}, pred[128,128]{0,1:T(8,128)(4,1)S(1)}, u32[]{:S(2)}) copy-start(pred[128,128]{0,1:T(8,128)(4,1)S(1)} %iota_compare_fusion) | copy-start | bytes 49156
  98.8 10.6 %collective-permute-start.1 = (f32[16,8320]{1,0:T(8,128)S(1)}, f32[16,8320]{1,0:T(8,128)S(1)}, u32[]{:S(2)}, u32[]{:S(2)}) collective-permute-start(f32[16,8320]{1,0:T(8,128)S(1)} %collective-permute-done), channel_id=1, source_target_pairs={{1,0},{2,1},{3,2},{4,3},{5,4},{6,5},{7,6},{8,7},{9,8},{10,9},{11,1... | collective-permute-start | bytes 1597448 | tf_op jit(solution)/shard_map/ppermute | solution.py:27
  104.4 10.6 %collective-permute-start.7 = (f32[16,8320]{1,0:T(8,128)S(1)}, f32[16,8320]{1,0:T(8,128)S(1)}, u32[]{:S(2)}, u32[]{:S(2)}) collective-permute-start(f32[16,8320]{1,0:T(8,128)S(1)} %collective-permute-done.6), channel_id=1, source_target_pairs={{0,1},{1,2},{2,3},{3,4},{4,5},{5,6},{6,7},{7,8},{8,9},{9,10},{10,1... | collective-permute-start | bytes 1597448 | tf_op jit(solution)/shard_map/ppermute | solution.py:27
  109.6 15.4 %collective-permute-start.2 = (f32[16,8320]{1,0:T(8,128)S(1)}, f32[16,8320]{1,0:T(8,128)S(1)}, u32[]{:S(2)}, u32[]{:S(2)}) collective-permute-start(f32[16,8320]{1,0:T(8,128)S(1)} %pad_maximum_fusion.2), channel_id=1, source_target_pairs={{2,0},{3,1},{4,2},{5,3},{6,4},{7,5},{8,6},{9,7},{10,8},{11,9},{12,... | collective-permute-start | bytes 1597448 | tf_op jit(solution)/shard_map/ppermute | solution.py:27
  115.2 15.3 %collective-permute-start.8 = (f32[16,8320]{1,0:T(8,128)S(1)}, f32[16,8320]{1,0:T(8,128)S(1)}, u32[]{:S(2)}, u32[]{:S(2)}) collective-permute-start(f32[16,8320]{1,0:T(8,128)S(1)} %pad_maximum_fusion.6), channel_id=1, source_target_pairs={{0,2},{1,3},{2,4},{3,5},{4,6},{5,7},{6,8},{7,9},{8,10},{9,11},{10,... | collective-permute-start | bytes 1597448 | tf_op jit(solution)/shard_map/ppermute | solution.py:27
  125.2 26.5 %collective-permute-start.3 = (f32[16,8320]{1,0:T(8,128)S(1)}, f32[16,8320]{1,0:T(8,128)S(1)}, u32[]{:S(2)}, u32[]{:S(2)}) collective-permute-start(f32[16,8320]{1,0:T(8,128)S(1)} %pad_maximum_fusion.3), channel_id=1, source_target_pairs={{4,0},{5,1},{6,2},{7,3},{8,4},{9,5},{10,6},{11,7},{12,8},{13,9},{1... | collective-permute-start | bytes 1597448 | tf_op jit(solution)/shard_map/ppermute | solution.py:27
  130.6 29.9 %collective-permute-start.9 = (f32[16,8320]{1,0:T(8,128)S(1)}, f32[16,8320]{1,0:T(8,128)S(1)}, u32[]{:S(2)}, u32[]{:S(2)}) collective-permute-start(f32[16,8320]{1,0:T(8,128)S(1)} %pad_maximum_fusion.7), channel_id=1, source_target_pairs={{0,4},{1,5},{2,6},{3,7},{4,8},{5,9},{6,10},{7,11},{8,12},{9,13},{1... | collective-permute-start | bytes 1597448 | tf_op jit(solution)/shard_map/ppermute | solution.py:27
  151.9 13.9 %collective-permute-start.4 = (f32[16,8320]{1,0:T(8,128)S(1)}, f32[16,8320]{1,0:T(8,128)S(1)}, u32[]{:S(2)}, u32[]{:S(2)}) collective-permute-start(f32[16,8320]{1,0:T(8,128)S(1)} %pad_maximum_fusion.4), channel_id=1, source_target_pairs={{8,0},{9,1},{10,2},{11,3},{12,4},{13,5},{14,6},{15,7},{16,8},{17,9... | collective-permute-start | bytes 1597448 | tf_op jit(solution)/shard_map/ppermute | solution.py:27
  160.5 26.0 %copy-start.1 = (bf16[128,1024]{0,1:T(8,128)(2,1)S(1)}, bf16[128,1024]{0,1:T(8,128)(2,1)}, u32[]{:S(2)}) copy-start(bf16[128,1024]{0,1:T(8,128)(2,1)} %get-tuple-element.75) | copy-start | bytes 786436
  160.7 13.2 %collective-permute-start.10 = (f32[16,8320]{1,0:T(8,128)S(1)}, f32[16,8320]{1,0:T(8,128)S(1)}, u32[]{:S(2)}, u32[]{:S(2)}) collective-permute-start(f32[16,8320]{1,0:T(8,128)S(1)} %pad_maximum_fusion.8), channel_id=1, source_target_pairs={{0,8},{1,9},{2,10},{3,11},{4,12},{5,13},{6,14},{7,15},{8,16},{9,17... | collective-permute-start | bytes 1597448 | tf_op jit(solution)/shard_map/ppermute | solution.py:27
  166.0 19.6 %collective-permute-start.5 = (f32[16,8320]{1,0:T(8,128)S(1)}, f32[16,8320]{1,0:T(8,128)S(1)}, u32[]{:S(2)}, u32[]{:S(2)}) collective-permute-start(f32[16,8320]{1,0:T(8,128)S(1)} %pad_maximum_fusion.5), channel_id=1, source_target_pairs={{16,0},{17,1},{18,2},{19,3},{20,4},{21,5},{22,6},{23,7},{24,8},{25... | collective-permute-start | bytes 1597448 | tf_op jit(solution)/shard_map/ppermute | solution.py:27
  174.1 14.2 %collective-permute-start.11 = (f32[16,8320]{1,0:T(8,128)S(1)}, f32[16,8320]{1,0:T(8,128)}, u32[]{:S(2)}, u32[]{:S(2)}) collective-permute-start(f32[16,8320]{1,0:T(8,128)S(1)} %pad_maximum_fusion.9), channel_id=1, source_target_pairs={{0,16},{1,17},{2,18},{3,19},{4,20},{5,21},{6,22},{7,23},{8,24},{9,... | collective-permute-start | bytes 1597448 | tf_op jit(solution)/shard_map/ppermute | solution.py:27
  209.5 189.4 %all-reduce.2.cloned.1.call-start = ((), (), s32[]{:S(2)}) async-start(), calls=%async_computation.2 | async-start | bytes 1310720 | tf_op jit(solution)/shard_map/psum | solution.py:179
Sparse Core Ops, SparseCore 0:
  209.7 113.0 reduce-scatter.3
  325.2 73.6 all-reduce.1
